TPU v7x, 128 devices: a whole 4x4x4 slice. The times are simulated.
128 devices in a mesh: dp: 8 (over z, core), ctx: 16 (over y, x).
Axes of the slice: x: 4, y: 4, z: 4, core: 2. Of those that a mesh axis runs over, the one named last changes fastest.
Arguments:
- queries: bfloat16 [8, 2048, 6144], P('dp', 'ctx'), may hold values from -6 to 6
- kv_proj: bfloat16 [8, 4096, 1024], P('dp', 'ctx'), may hold values from -6 to 6
- hidden: bfloat16 [8, 4096, 12288], P('dp', 'ctx'), may hold values from -0.119628906 to 0.119628906
- grad_out: bfloat16 [8, 2048, 6144], P('dp', 'ctx'), may hold values from -6 to 6
- doc_lengths: int32 [8, 256], P('dp'), may hold values from 1 to 8192, 262144 in all within a row
- slab_offsets: int32 [8], P('dp'), may hold values from 0 to 260096
Outputs:
- attended: bfloat16 [8, 2048, 6144], P('dp', 'ctx')
- grad_queries: bfloat16 [8, 2048, 6144], P('dp', 'ctx')
- grad_kv: bfloat16 [8, 4096, 1024], P('dp', 'ctx')
- grad_weight: float32 [12288, 1024], P('ctx', 'dp')
All inputs are finite; a program needn't handle non-finite values.
Results may differ from a plain program's by a relative error of at most 0.025.
Values may be sent and summed in bfloat16 or wider, within the bound.
No kernel may reach another device: no remote copies, remote signals or barrier semaphores. Data moves between devices by JAX's collectives and lax.ppermute only.
A program may use at most 192 MiB of HBM per device.

v0:
```python
import functools

import jax
import jax.numpy as jnp
from jax import lax
from jax.experimental import pallas as pl
from jax.experimental.pallas import tpu as pltpu
from jax.sharding import PartitionSpec as P


HEAD_FEATURES = 128
KEY_VALUE_HEADS = 4
WINDOW = 2048
BLOCK_QUERIES = 256
CTX_ROWS = 4


def doc_index(positions, bounds):
    return jnp.sum(
        (bounds[None, :] <= positions[:, None]).astype(jnp.int32), axis=1, dtype=jnp.int32
    )


def attention_kernel(qdoc_ref, kdoc_ref, q_ref, go_ref, kv_ref, att_ref, dq_ref, dkv_ref, *, bq, span, heads):
    qb = pl.program_id(0)
    f32 = jnp.float32
    bf16 = jnp.bfloat16
    factor = HEAD_FEATURES ** (-0.5)

    @pl.when(qb == 0)
    def _():
        dkv_ref[...] = jnp.zeros_like(dkv_ref)

    start = pl.multiple_of(qb * bq, bq)
    k = kv_ref[pl.ds(start, span), 0:HEAD_FEATURES]
    v = kv_ref[pl.ds(start, span), HEAD_FEATURES : 2 * HEAD_FEATURES]
    nt = (((1,), (1,)), ((), ()))
    tn = (((0,), (0,)), ((), ()))
    row = lax.broadcasted_iota(jnp.int32, (bq, span), 0)
    col = lax.broadcasted_iota(jnp.int32, (bq, span), 1)
    same_doc = qdoc_ref[...] == kdoc_ref[:, pl.ds(start, span)]
    allowed = (col > row) & (col <= row + WINDOW) & same_doc
    for h in range(heads):
        cols = slice(h * HEAD_FEATURES, (h + 1) * HEAD_FEATURES)
        q = q_ref[:, cols]
        go = go_ref[:, cols]
        scores = lax.dot_general(q, k, nt, preferred_element_type=f32) * factor
        scores = jnp.where(allowed, scores, -1e30)
        maxima = jnp.max(scores, axis=1, keepdims=True)
        raised = jnp.exp(scores - maxima)
        weights = raised * (1.0 / jnp.sum(raised, axis=1, keepdims=True))
        weights_low = weights.astype(bf16)
        att = jnp.dot(weights_low, v, preferred_element_type=f32).astype(bf16)
        att_ref[:, cols] = att
        grad_probs = lax.dot_general(go, v, nt, preferred_element_type=f32)
        deltas = jnp.sum(go.astype(f32) * att.astype(f32), axis=1, keepdims=True)
        grad_scores = (weights * (grad_probs - deltas) * factor).astype(bf16)
        dq_ref[:, cols] = jnp.dot(grad_scores, k, preferred_element_type=f32).astype(bf16)
        dk = lax.dot_general(q, grad_scores, tn, preferred_element_type=f32)
        dv = lax.dot_general(go, weights_low, tn, preferred_element_type=f32)
        dkv_ref[0:HEAD_FEATURES, pl.ds(start, span)] += dk
        dkv_ref[HEAD_FEATURES : 2 * HEAD_FEATURES, pl.ds(start, span)] += dv


def head_attention(head_queries, head_upstream, head_keys, q_doc, k_doc):
    rows = head_queries.shape[0]
    keys = head_keys.shape[0]
    heads_here = head_queries.shape[1] // HEAD_FEATURES
    bq = min(BLOCK_QUERIES, rows)
    span = bq + WINDOW
    grid = (rows // bq,)
    kernel = functools.partial(attention_kernel, bq=bq, span=span, heads=heads_here)
    width = heads_here * HEAD_FEATURES
    flops = 12 * heads_here * rows * span * HEAD_FEATURES
    bytes_accessed = 2 * (4 * rows * heads_here * HEAD_FEATURES + keys * 2 * HEAD_FEATURES) + 4 * keys * 2 * HEAD_FEATURES
    return pl.pallas_call(
        kernel,
        grid=grid,
        in_specs=[
            pl.BlockSpec((bq, 1), lambda i: (i, 0)),
            pl.BlockSpec((1, keys), lambda i: (0, 0)),
            pl.BlockSpec((bq, width), lambda i: (i, 0)),
            pl.BlockSpec((bq, width), lambda i: (i, 0)),
            pl.BlockSpec((keys, 2 * HEAD_FEATURES), lambda i: (0, 0)),
        ],
        out_specs=[
            pl.BlockSpec((bq, width), lambda i: (i, 0)),
            pl.BlockSpec((bq, width), lambda i: (i, 0)),
            pl.BlockSpec((2 * HEAD_FEATURES, keys), lambda i: (0, 0)),
        ],
        out_shape=[
            jax.ShapeDtypeStruct(head_queries.shape, jnp.bfloat16),
            jax.ShapeDtypeStruct(head_queries.shape, jnp.bfloat16),
            jax.ShapeDtypeStruct((2 * HEAD_FEATURES, keys), jnp.float32),
        ],
        compiler_params=pltpu.CompilerParams(
            dimension_semantics=("arbitrary",),
            vmem_limit_bytes=60 * 1024 * 1024,
        ),
        cost_estimate=pl.CostEstimate(
            flops=flops, transcendentals=heads_here * rows * span, bytes_accessed=bytes_accessed
        ),
        name="band_attention",
    )(q_doc.reshape(rows, 1), k_doc.reshape(1, keys), head_queries, head_upstream, head_keys)


def weight_kernel(me_ref, *refs, parts):
    pieces, grad_ref, out_ref = refs[:parts], refs[parts], refs[parts + 1]
    me = me_ref[0]
    total = None
    for shift in range(parts):
        source = lax.rem(me - shift + parts, parts)
        term = lax.dot_general(
            pieces[shift][...], grad_ref[source], (((0,), (0,)), ((), ())),
            preferred_element_type=jnp.float32,
        )
        total = term if total is None else total + term
    out_ref[...] = total.astype(out_ref.dtype)


def stacked_weight_product(me, pieces, grad_all):
    parts = len(pieces)
    rows, width = pieces[0].shape
    columns = grad_all.shape[2]
    tile = 512 if width % 512 == 0 else width
    grid_spec = pltpu.PrefetchScalarGridSpec(
        num_scalar_prefetch=1,
        grid=(width // tile,),
        in_specs=[pl.BlockSpec((rows, tile), lambda i, me: (0, i)) for _ in range(parts)]
        + [pl.BlockSpec((parts, rows, columns), lambda i, me: (0, 0, 0))],
        out_specs=pl.BlockSpec((tile, columns), lambda i, me: (i, 0)),
    )
    return pl.pallas_call(
        functools.partial(weight_kernel, parts=parts),
        grid_spec=grid_spec,
        out_shape=jax.ShapeDtypeStruct((width, columns), jnp.bfloat16),
        compiler_params=pltpu.CompilerParams(
            dimension_semantics=("arbitrary",), vmem_limit_bytes=48 * 1024 * 1024
        ),
        cost_estimate=pl.CostEstimate(
            flops=2 * parts * rows * width * columns,
            transcendentals=0,
            bytes_accessed=2 * parts * rows * (width + columns) + 2 * width * columns,
        ),
        name="weight_product",
    )(jnp.reshape(me, (1,)).astype(jnp.int32), *pieces, grad_all)


def send_hidden(hidden_rows):
    dp = lax.axis_size("dp")
    ctx = lax.axis_size("ctx")
    rows, features = hidden_rows.shape
    piece = features // (ctx * dp)
    width = features // dp
    me = lax.axis_index("dp")
    across = ctx // CTX_ROWS
    interleaved = (
        hidden_rows.reshape(rows, CTX_ROWS, across, dp, piece)
        .transpose(3, 0, 2, 1, 4)
        .reshape(dp, rows, width)
    )
    received = [lax.dynamic_index_in_dim(interleaved, me, 0, keepdims=False)]
    for shift in range(1, dp):
        outgoing = lax.dynamic_index_in_dim(interleaved, (me + shift) % dp, 0, keepdims=False)
        pairs = [(i, (i + shift) % dp) for i in range(dp)]
        received.append(lax.ppermute(outgoing, "dp", pairs))
    return me, received


def weight_gradient(me, received, grad_all, grad_query_heads):
    partial = stacked_weight_product(me, received, grad_all)
    ctx = lax.axis_size("ctx")
    across = ctx // CTX_ROWS
    along_x = [[y * across + x for x in range(across)] for y in range(CTX_ROWS)]
    along_y = [[y * across + x for y in range(CTX_ROWS)] for x in range(across)]
    reduced = lax.psum_scatter(partial, "ctx", scatter_dimension=0, axis_index_groups=along_x, tiled=True)
    reduced, grad_query_heads = lax.optimization_barrier((reduced, grad_query_heads))
    grad_query = lax.all_to_all(grad_query_heads, "ctx", split_axis=0, concat_axis=1, tiled=True)
    reduced = lax.psum_scatter(reduced, "ctx", scatter_dimension=0, axis_index_groups=along_y, tiled=True)
    weight = lax.all_to_all(reduced.astype(jnp.float32), "dp", split_axis=1, concat_axis=0, tiled=True)
    return weight, grad_query


def local_body(queries, kv_proj, hidden, grad_out, doc_lengths, slab_offsets):
    query_matrix_rows = queries[0]
    upstream_gradient = grad_out[0]
    key_matrix_rows = kv_proj[0]
    hidden_rows = hidden[0]
    bounds = jnp.cumsum(doc_lengths[0], dtype=jnp.int32)
    offset = slab_offsets[0]
    key_value_width = 2 * KEY_VALUE_HEADS * HEAD_FEATURES
    repeat_heads = lax.axis_size("ctx") // KEY_VALUE_HEADS
    key_total_count = key_matrix_rows.shape[0]
    copies = jnp.broadcast_to(
        key_matrix_rows.reshape(key_total_count, KEY_VALUE_HEADS, 1, 2 * HEAD_FEATURES),
        (key_total_count, KEY_VALUE_HEADS, repeat_heads, 2 * HEAD_FEATURES),
    ).reshape(key_total_count, KEY_VALUE_HEADS * repeat_heads * 2 * HEAD_FEATURES)
    head_queries, head_upstream, head_keys = (
        lax.all_to_all(query_matrix_rows, "ctx", split_axis=1, concat_axis=0, tiled=True),
        lax.all_to_all(upstream_gradient, "ctx", split_axis=1, concat_axis=0, tiled=True),
        lax.all_to_all(copies, "ctx", split_axis=1, concat_axis=0, tiled=True),
    )
    me, received = send_hidden(hidden_rows)
    rows = head_queries.shape[0]
    keys = head_keys.shape[0]
    query_pos = offset + jnp.arange(rows, dtype=jnp.int32)
    key_pos = offset - WINDOW + jnp.arange(keys, dtype=jnp.int32)
    q_doc = doc_index(query_pos, bounds)
    k_doc = jnp.where(key_pos >= 0, doc_index(key_pos, bounds), -1)
    attended_heads, grad_query_heads, grad_head = head_attention(head_queries, head_upstream, head_keys, q_doc, k_doc)
    attended = lax.all_to_all(attended_heads, "ctx", split_axis=0, concat_axis=1, tiled=True)
    partial_sums = lax.all_to_all(
        grad_head.T.astype(jnp.bfloat16), "ctx", split_axis=0, concat_axis=1, tiled=True
    )
    grad_keys = jnp.sum(
        partial_sums.reshape(
            partial_sums.shape[0], KEY_VALUE_HEADS, repeat_heads, 2 * HEAD_FEATURES
        ).astype(jnp.float32),
        axis=2,
    ).reshape(partial_sums.shape[0], key_value_width)
    grad_low = grad_keys.astype(jnp.bfloat16)
    grad_all = lax.all_gather(grad_low, "dp", axis=0, tiled=False)
    attended, grad_all = lax.optimization_barrier((attended, grad_all))
    grad_weight, grad_query = weight_gradient(me, received, grad_all, grad_query_heads)
    return (attended[None], grad_query[None], grad_low[None], grad_weight)


def solution(mesh):
    in_specs = (
        P("dp", "ctx", None),
        P("dp", "ctx", None),
        P("dp", "ctx", None),
        P("dp", "ctx", None),
        P("dp", None),
        P("dp"),
    )
    out_specs = (P("dp", "ctx", None), P("dp", "ctx", None), P("dp", "ctx", None), P("ctx", "dp"))
    return jax.shard_map(local_body, mesh=mesh, in_specs=in_specs, out_specs=out_specs, check_vma=False)
```

profile of v0, /device:TPU:0, one launch (start us, length us, event | category | flops | bytes accessed | tf_op | source)
XLA Modules:
  0.0 409.9 jit_solution(12837300700131519770)
XLA Ops:
  7.2 1.7 copy.101
  8.9 1.5 copy.75
  10.4 7.3 %all-to-all-start = ((bf16[128,16,384]{2,0,1:T(8,128)(2,1)}), bf16[128,16,384]{2,0,1:T(8,128)(2,1)S(1)}, u32[]{:S(2)}, u32[]{:S(2)}) async-start(bf16[128,16,384]{2,0,1:T(8,128)(2,1)} %copy.75), calls=%async_computation | async-start | bytes 3145728 | tf_op jit(solution)/shard_map/all_to_all | solution.py:199
  18.0 1.5 copy.76
  19.5 22.7 %all-to-all-done = bf16[128,16,384]{2,0,1:T(8,128)(2,1)S(1)} async-done(((bf16[128,16,384]{2,0,1:T(8,128)(2,1)}), bf16[128,16,384]{2,0,1:T(8,128)(2,1)S(1)}, u32[]{:S(2)}, u32[]{:S(2)}) %all-to-all-start) | async-done | bytes 1572896 | tf_op jit(solution)/shard_map/all_to_all | solution.py:199
  42.2 4.4 %all-to-all-start.1 = ((bf16[128,16,384]{2,0,1:T(8,128)(2,1)}), bf16[128,16,384]{2,0,1:T(8,128)(2,1)}, u32[]{:S(2)}, u32[]{:S(2)}) async-start(bf16[128,16,384]{2,0,1:T(8,128)(2,1)} %copy.76), calls=%async_computation.1 | async-start | bytes 3145728 | tf_op jit(solution)/shard_map/all_to_all | solution.py:200
  47.1 21.7 %all-to-all-done.1 = bf16[128,16,384]{2,0,1:T(8,128)(2,1)} async-done(((bf16[128,16,384]{2,0,1:T(8,128)(2,1)}), bf16[128,16,384]{2,0,1:T(8,128)(2,1)}, u32[]{:S(2)}, u32[]{:S(2)}) %all-to-all-start.1) | async-done | bytes 1572896 | tf_op jit(solution)/shard_map/all_to_all | solution.py:200
  68.8 1.5 broadcast_in_dim.24
  70.3 3.8 all-to-all-start.2
  76.3 1.4 copy.78.qdoc_ref
  77.8 1.3 convert_reduce_fusion
  79.7 23.6 %all-to-all-done.2 = bf16[256,16,256]{2,0,1:T(8,128)(2,1)S(1)} async-done(((bf16[256,16,256]{2,0,1:T(8,128)(2,1)}), bf16[256,16,256]{2,0,1:T(8,128)(2,1)S(1)}, u32[]{:S(2)}, u32[]{:S(2)}) %all-to-all-start.2) | async-done | bytes 2097184 | tf_op jit(solution)/shard_map/all_to_all | solution.py:201
  103.3 1.3 copy-done
  104.6 61.2 %band_attention.1 = (bf16[2048,384]{1,0:T(8,128)(2,1)}, bf16[2048,384]{1,0:T(8,128)(2,1)}, f32[256,4096]{1,0:T(8,128)}) custom-call(s32[2048,1]{1,0:T(8,128)} %copy.78.qdoc_ref, s32[1,4096]{1,0:T(1,128)} %compare_select_fusion.kdoc_ref, bf16[2048,384]{1,0:T(8,128)(2,1)} %bitcast.76, bf16[2048,384]{1,0:T(8,128)(2,1)} %bitcast.8.go_ref, bf16[4096,256]{1,0:T(8,128)(2,1)} %bitcast.71), custom_call_target="tpu_custom_call" | custom-call | flops 21743271936 | bytes 12582912 | tf_op jit(solution)/shard_map/band_attention/pallas_call | solution.py:76
  165.8 2.5 convert_element_type.37
  168.5 31.4 %all_to_all.130 = bf16[16,256,256]{1,2,0:T(8,128)(2,1)S(1)} all-to-all(bf16[16,256,256]{1,2,0:T(8,128)(2,1)S(1)} %bitcast.66), channel_id=1, replica_groups=mesh['dp'=8,'ctx'=16] {'ctx'}, dimensions={0} | all-to-all | bytes 4194304 | tf_op jit(solution)/shard_map/all_to_all | solution.py:212
  200.2 1.0 copy.83
  201.3 8.7 %copy.84 = bf16[1,256,12288]{1,2,0:T(8,128)(2,1)} copy(bf16[1,256,12288]{2,1,0:T(8,128)(2,1)} %param.8) | data formatting | bytes 12582912 | tf_op args[2]
  210.0 6.3 %copy.85 = bf16[8,256,4,4,96]{1,4,3,2,0:T(8,128)(2,1)} copy(bf16[8,256,4,4,96]{1,4,0,2,3:T(8,128)(2,1)} %bitcast.64) | data formatting | bytes 12582912 | tf_op jit(solution)/shard_map/transpose | solution.py:159
  216.3 4.7 %constant_dynamic-slice_fusion = (bf16[1,256,1536]{1,2,0:T(8,128)(2,1)S(1)}, bf16[1,256,1536]{1,2,0:T(8,128)(2,1)}, bf16[1,256,1536]{1,2,0:T(8,128)(2,1)}, bf16[...) fusion(bf16[8,256,1536]{1,2,0:T(8,128)(2,1)} %bitcast.63, ...), kind=kLoop, calls=%fused_computation.9 | loop fusion | bytes 12582944 | tf_op jit(solution)/shard_map/jit(dynamic_index_in_dim)/dynamic_slice | solution.py:164
  221.0 1.2 copy.87
  222.2 1.2 copy.88
  223.4 1.8 collective-permute-start.1
  225.2 4.4 %all-to-all-start.3 = ((bf16[16,128,384]{2,1,0:T(8,128)(2,1)}), bf16[16,128,384]{2,1,0:T(8,128)(2,1)}, u32[]{:S(2)}, u32[]{:S(2)}) async-start(bf16[16,128,384]{2,1,0:T(8,128)(2,1)} %bitcast.74), calls=%async_computation.3 | async-start | bytes 3145728 | tf_op jit(solution)/shard_map/all_to_all | solution.py:211
  229.6 1.1 copy.89
  230.8 2.9 collective-permute-start.2
  233.7 2.3 copy.90
  235.9 1.2 collective-permute-start.3
  237.2 2.3 copy.91
  239.5 2.3 collective-permute-start.4
  241.8 2.4 copy.92
  244.2 1.2 copy.93
  245.3 1.3 collective-permute-done.refs_1_
  248.1 16.2 %collective-permute-start.6 = (bf16[256,1536]{1,0:T(8,128)(2,1)}, bf16[256,1536]{1,0:T(8,128)(2,1)}, u32[]{:S(2)}, u32[]{:S(2)}) collective-permute-start(bf16[256,1536]{1,0:T(8,128)(2,1)} %bitcast.81), channel_id=1, source_target_pairs={{0,112},{16,0},{32,16},{48,32},{64,48},{80,64},{96,80},{112,96},{1... | collective-permute-start | bytes 2359304 | tf_op jit(solution)/shard_map/ppermute | solution.py:166
  264.2 1.4 copy.86
  265.7 2.8 copy.100
  268.5 12.2 %collective-permute-done.2.refs_3_ = bf16[256,1536]{1,0:T(8,128)(2,1)S(1)} collective-permute-done((bf16[256,1536]{1,0:T(8,128)(2,1)}, bf16[256,1536]{1,0:T(8,128)(2,1)S(1)}, u32[]{:S(2)}, u32[]{:S(2)}) %collective-permute-start.2) | collective-permute-done | bytes 786464 | tf_op jit(solution)/shard_map/ppermute | solution.py:166
  280.7 1.2 collective-permute-done.3.refs_4_
  281.9 12.9 %collective-permute-done.4.refs_5_ = bf16[256,1536]{1,0:T(8,128)(2,1)} collective-permute-done((bf16[256,1536]{1,0:T(8,128)(2,1)}, bf16[256,1536]{1,0:T(8,128)(2,1)}, u32[]{:S(2)}, u32[]{:S(2)}) %collective-permute-start.4) | collective-permute-done | bytes 786464 | tf_op jit(solution)/shard_map/ppermute | solution.py:166
  294.8 6.8 %collective-permute-done.6.refs_7_ = bf16[256,1536]{1,0:T(8,128)(2,1)} collective-permute-done((bf16[256,1536]{1,0:T(8,128)(2,1)}, bf16[256,1536]{1,0:T(8,128)(2,1)}, u32[]{:S(2)}, u32[]{:S(2)}) %collective-permute-start.6) | collective-permute-done | bytes 786464 | tf_op jit(solution)/shard_map/ppermute | solution.py:166
  301.6 10.8 %weight_product.1 = bf16[1536,1024]{1,0:T(8,128)(2,1)} custom-call(s32[1]{0:T(128)} %bitcast.19.me_ref, bf16[256,1536]{1,0:T(8,128)(2,1)S(1)} %bitcast.62, bf16[256,1536]{1,0:T(8,128)(2,1)S(1)} %collective-permute-done.refs_1_, bf16[256,1536]{1,0:T(8,128)(2,1)S(1)} %collective-permute-done.1.refs_2_, bf16[256,1536]{1,0:T(8,128)(2,1)S(1)} %collective-permute-done.2.refs_3_, ...), custom_call_target="tpu_custom_call" | custom-call | flops 6442450944 | bytes 13631488 | tf_op jit(solution)/shard_map/weight_product/pallas_call | solution.py:133
  312.5 40.1 %reduce-scatter.3.cloned.1.call-done = bf16[384,1024]{1,0:T(8,128)(2,1)} async-done(((bf16[1536,1024]{1,0:T(8,128)(2,1)}), bf16[384,1024]{1,0:T(8,128)(2,1)}) %reduce-scatter.3.cloned.1.call-update) | async-done | bytes 786448 | tf_op jit(solution)/shard_map/reduce_scatter | solution.py:176
  352.6 5.3 %all-to-all-start.5 = ((bf16[16,128,384]{2,1,0:T(8,128)(2,1)}), bf16[16,128,384]{2,1,0:T(8,128)(2,1)S(1)}, u32[]{:S(2)}, u32[]{:S(2)}) async-start(bf16[16,128,384]{2,1,0:T(8,128)(2,1)} %bitcast.31), calls=%async_computation.6 | async-start | bytes 3145728 | tf_op jit(solution)/shard_map/all_to_all | solution.py:178
  357.9 29.6 %reduce-scatter.5.cloned.1.call-done = bf16[96,1024]{1,0:T(8,128)(2,1)} async-done(((bf16[384,1024]{1,0:T(8,128)(2,1)}), bf16[96,1024]{1,0:T(8,128)(2,1)}) %reduce-scatter.5.cloned.1.call-update) | async-done | bytes 196624 | tf_op jit(solution)/shard_map/reduce_scatter | solution.py:179
  387.6 1.7 copy_bitcast_fusion.1
  389.3 4.4 %all-to-all-start.6 = ((f32[96,8,128]{2,0,1:T(8,128)}), f32[96,8,128]{2,0,1:T(8,128)S(1)}, u32[]{:S(2)}, u32[]{:S(2)}) async-start(f32[96,8,128]{2,0,1:T(8,128)} %copy_bitcast_fusion.1), calls=%async_computation.8 | async-start | bytes 786432 | tf_op jit(solution)/shard_map/all_to_all | solution.py:180
  394.6 1.6 broadcast_in_dim.26
  396.3 6.4 %all-to-all-done.6 = f32[96,8,128]{2,0,1:T(8,128)S(1)} async-done(((f32[96,8,128]{2,0,1:T(8,128)}), f32[96,8,128]{2,0,1:T(8,128)S(1)}, u32[]{:S(2)}, u32[]{:S(2)}) %all-to-all-start.6) | async-done | bytes 393248 | tf_op jit(solution)/shard_map/all_to_all | solution.py:180
  (38 shorter events, 6.6 us)
Async XLA Ops:
  10.4 7.3 %copy-start.1 = (bf16[1,128,6144]{2,1,0:T(8,128)(2,1)S(1)}, bf16[1,128,6144]{2,1,0:T(8,128)(2,1)}, u32[]{:S(2)}) copy-start(bf16[1,128,6144]{2,1,0:T(8,128)(2,1)} %param.9) | copy-start | bytes 4718596
  10.4 31.8 %all-to-all-start = ((bf16[128,16,384]{2,0,1:T(8,128)(2,1)}), bf16[128,16,384]{2,0,1:T(8,128)(2,1)S(1)}, u32[]{:S(2)}, u32[]{:S(2)}) async-start(bf16[128,16,384]{2,0,1:T(8,128)(2,1)} %copy.75), calls=%async_computation | async-start | bytes 3145728 | tf_op jit(solution)/shard_map/all_to_all | solution.py:199
  19.5 27.1 %copy-start.3 = (bf16[1,256,1024]{2,1,0:T(8,128)(2,1)S(1)}, bf16[1,256,1024]{2,1,0:T(8,128)(2,1)}, u32[]{:S(2)}) copy-start(bf16[1,256,1024]{2,1,0:T(8,128)(2,1)} %param.7) | copy-start | bytes 1572868
  42.2 4.8 %copy-start.2 = (bf16[128,16,384]{2,0,1:T(8,128)(2,1)}, bf16[128,16,384]{2,0,1:T(8,128)(2,1)S(1)}, u32[]{:S(2)}) copy-start(bf16[128,16,384]{2,0,1:T(8,128)(2,1)S(1)} %all-to-all-done) | copy-start | bytes 4718596
  42.2 26.6 %all-to-all-start.1 = ((bf16[128,16,384]{2,0,1:T(8,128)(2,1)}), bf16[128,16,384]{2,0,1:T(8,128)(2,1)}, u32[]{:S(2)}, u32[]{:S(2)}) async-start(bf16[128,16,384]{2,0,1:T(8,128)(2,1)} %copy.76), calls=%async_computation.1 | async-start | bytes 3145728 | tf_op jit(solution)/shard_map/all_to_all | solution.py:200
  70.3 4.1 copy-start.4
  70.3 32.9 %all-to-all-start.2 = ((bf16[256,16,256]{2,0,1:T(8,128)(2,1)}), bf16[256,16,256]{2,0,1:T(8,128)(2,1)S(1)}, u32[]{:S(2)}, u32[]{:S(2)}) async-start(bf16[256,16,256]{2,0,1:T(8,128)(2,1)} %bitcast.9), calls=%async_computation.2 | async-start | bytes 4194304 | tf_op jit(solution)/shard_map/all_to_all | solution.py:201
  74.2 194.3 %all-gather.2.cloned.1.call-start = ((), (), s32[]{:S(2)}) async-start(), calls=%async_computation.9 | async-start | bytes 4718592 | tf_op jit(solution)/shard_map/all_gather | solution.py:222
  103.3 1.3 copy-start
  222.2 24.4 %collective-permute-start = (bf16[256,1536]{1,0:T(8,128)(2,1)}, bf16[256,1536]{1,0:T(8,128)(2,1)S(1)}, u32[]{:S(2)}, u32[]{:S(2)}) collective-permute-start(bf16[256,1536]{1,0:T(8,128)(2,1)} %bitcast.84), channel_id=1, source_target_pairs={{0,16},{16,32},{32,48},{48,64},{64,80},{80,96},{96,112},{112,0},{1... | collective-permute-start | bytes 2359304 | tf_op jit(solution)/shard_map/ppermute | solution.py:166
  223.4 24.7 %collective-permute-start.1 = (bf16[256,1536]{1,0:T(8,128)(2,1)}, bf16[256,1536]{1,0:T(8,128)(2,1)S(1)}, u32[]{:S(2)}, u32[]{:S(2)}) collective-permute-start(bf16[256,1536]{1,0:T(8,128)(2,1)} %bitcast.83), channel_id=1, source_target_pairs={{0,32},{16,48},{32,64},{48,80},{64,96},{80,112},{96,0},{112,16},{1... | collective-permute-start | bytes 2359304 | tf_op jit(solution)/shard_map/ppermute | solution.py:166
  225.2 40.5 %all-to-all-start.3 = ((bf16[16,128,384]{2,1,0:T(8,128)(2,1)}), bf16[16,128,384]{2,1,0:T(8,128)(2,1)}, u32[]{:S(2)}, u32[]{:S(2)}) async-start(bf16[16,128,384]{2,1,0:T(8,128)(2,1)} %bitcast.74), calls=%async_computation.3 | async-start | bytes 3145728 | tf_op jit(solution)/shard_map/all_to_all | solution.py:211
  229.6 123.0 %reduce-scatter.3.cloned.1.call-start = ((), (), s32[]{:S(2)}) async-start(), calls=%async_computation.10 | async-start | bytes 3932160 | tf_op jit(solution)/shard_map/reduce_scatter | solution.py:176
  230.8 49.9 %collective-permute-start.2 = (bf16[256,1536]{1,0:T(8,128)(2,1)}, bf16[256,1536]{1,0:T(8,128)(2,1)S(1)}, u32[]{:S(2)}, u32[]{:S(2)}) collective-permute-start(bf16[256,1536]{1,0:T(8,128)(2,1)} %bitcast.78), channel_id=1, source_target_pairs={{0,48},{16,64},{32,80},{48,96},{64,112},{80,0},{96,16},{112,32},{1... | collective-permute-start | bytes 2359304 | tf_op jit(solution)/shard_map/ppermute | solution.py:166
  235.9 45.9 %collective-permute-start.3 = (bf16[256,1536]{1,0:T(8,128)(2,1)}, bf16[256,1536]{1,0:T(8,128)(2,1)}, u32[]{:S(2)}, u32[]{:S(2)}) collective-permute-start(bf16[256,1536]{1,0:T(8,128)(2,1)} %bitcast.79), channel_id=1, source_target_pairs={{0,64},{16,80},{32,96},{48,112},{64,0},{80,16},{96,32},{112,48},{1... | collective-permute-start | bytes 2359304 | tf_op jit(solution)/shard_map/ppermute | solution.py:166
  239.5 55.3 %collective-permute-start.4 = (bf16[256,1536]{1,0:T(8,128)(2,1)}, bf16[256,1536]{1,0:T(8,128)(2,1)}, u32[]{:S(2)}, u32[]{:S(2)}) collective-permute-start(bf16[256,1536]{1,0:T(8,128)(2,1)} %bitcast.80), channel_id=1, source_target_pairs={{0,80},{16,96},{32,112},{48,0},{64,16},{80,32},{96,48},{112,64},{1... | collective-permute-start | bytes 2359304 | tf_op jit(solution)/shard_map/ppermute | solution.py:166
  246.6 48.2 %collective-permute-start.5 = (bf16[256,1536]{1,0:T(8,128)(2,1)}, bf16[256,1536]{1,0:T(8,128)(2,1)}, u32[]{:S(2)}, u32[]{:S(2)}) collective-permute-start(bf16[256,1536]{1,0:T(8,128)(2,1)} %bitcast.82), channel_id=1, source_target_pairs={{0,96},{16,112},{32,0},{48,16},{64,32},{80,48},{96,64},{112,80},{1... | collective-permute-start | bytes 2359304 | tf_op jit(solution)/shard_map/ppermute | solution.py:166
  248.1 53.6 %collective-permute-start.6 = (bf16[256,1536]{1,0:T(8,128)(2,1)}, bf16[256,1536]{1,0:T(8,128)(2,1)}, u32[]{:S(2)}, u32[]{:S(2)}) collective-permute-start(bf16[256,1536]{1,0:T(8,128)(2,1)} %bitcast.81), channel_id=1, source_target_pairs={{0,112},{16,0},{32,16},{48,32},{64,48},{80,64},{96,80},{112,96},{1... | collective-permute-start | bytes 2359304 | tf_op jit(solution)/shard_map/ppermute | solution.py:166
  312.4 75.1 %reduce-scatter.5.cloned.1.call-start = ((), (), s32[]{:S(2)}) async-start(), calls=%async_computation.11 | async-start | bytes 983040 | tf_op jit(solution)/shard_map/reduce_scatter | solution.py:179
  352.6 36.7 %all-to-all-start.5 = ((bf16[16,128,384]{2,1,0:T(8,128)(2,1)}), bf16[16,128,384]{2,1,0:T(8,128)(2,1)S(1)}, u32[]{:S(2)}, u32[]{:S(2)}) async-start(bf16[16,128,384]{2,1,0:T(8,128)(2,1)} %bitcast.31), calls=%async_computation.6 | async-start | bytes 3145728 | tf_op jit(solution)/shard_map/all_to_all | solution.py:178
  389.3 13.3 %all-to-all-start.6 = ((f32[96,8,128]{2,0,1:T(8,128)}), f32[96,8,128]{2,0,1:T(8,128)S(1)}, u32[]{:S(2)}, u32[]{:S(2)}) async-start(f32[96,8,128]{2,0,1:T(8,128)} %copy_bitcast_fusion.1), calls=%async_computation.8 | async-start | bytes 786432 | tf_op jit(solution)/shard_map/all_to_all | solution.py:180
Sparse Core Ops, SparseCore 0:
  201.3 34.0 all-gather.1
  312.6 39.9 reduce-scatter.2
  355.0 32.5 reduce-scatter.4
where the time goes:
time: 411 us; the launch traced here: 410 us
  waiting for transfers between devices  179 us (44%)
  Pallas kernels  72 us (18%)
  starting transfers between devices  55.4 us (13%)
  local copies, waits for them, and re-layouts  50.1 us (12%)
  blocking collectives  31.4 us (8%)
  between operations  14.7 us (4%)
  other arithmetic  7.43 us (2%)
    pallas_call x1, Pallas kernels, head_attention(): pl.pallas_call(kernel, grid=grid, in_specs=[pl.BlockSpec((bq, 1), lambda...  61.2 us
    reduce_scatter x1, waiting for transfers between devices, weight_gradient(): lax.psum_scatter(partial, 'ctx', scatter_dimension=0, axis_index_groups=a...  40.1 us
    ppermute x7, waiting for transfers between devices, send_hidden(): received.append(lax.ppermute(outgoing, 'dp', pairs))  34.9 us
    all_to_all x1, blocking collectives, local_body(): lax.all_to_all(grad_head.T.astype(jnp.bfloat16), 'ctx', split_axis=0, con...  31.4 us
    reduce_scatter x1, waiting for transfers between devices, weight_gradient(): lax.psum_scatter(reduced, 'ctx', scatter_dimension=0, axis_index_groups=a...  29.6 us
    ppermute x7, starting transfers between devices, send_hidden(): received.append(lax.ppermute(outgoing, 'dp', pairs))  25.4 us
    all_to_all x1, waiting for transfers between devices, local_body(): lax.all_to_all(copies, 'ctx', split_axis=1, concat_axis=0, tiled=True)  23.6 us
    all_to_all x1, waiting for transfers between devices, local_body(): lax.all_to_all(query_matrix_rows, 'ctx', split_axis=1, concat_axis=0, til...  22.7 us
  transfers between devices with their start and end apart: 16, of which 12 were waited for; matrix products, arithmetic and copies ran while one was open for 11% of the time, Pallas kernels for 0%

commit v1 on v0

--- a/solution.py
+++ b/solution.py
@@ -11,7 +11,7 @@
 HEAD_FEATURES = 128
 KEY_VALUE_HEADS = 4
 WINDOW = 2048
-BLOCK_QUERIES = 256
+BLOCK_QUERIES = 512
 CTX_ROWS = 4
 
 
@@ -94,8 +94,7 @@
             jax.ShapeDtypeStruct((2 * HEAD_FEATURES, keys), jnp.float32),
         ],
         compiler_params=pltpu.CompilerParams(
-            dimension_semantics=("arbitrary",),
-            vmem_limit_bytes=60 * 1024 * 1024,
+            dimension_semantics=("arbitrary",), vmem_limit_bytes=60 * 1024 * 1024
         ),
         cost_estimate=pl.CostEstimate(
             flops=flops, transcendentals=heads_here * rows * span, bytes_accessed=bytes_accessed

time: 411 us -> 413 us (level)
  no operation moved by 1% of the time
where the time goes in v1:
time: 413 us; the launch traced here: 412 us
  waiting for transfers between devices  179 us (43%)
  Pallas kernels  74 us (18%)
  starting transfers between devices  55.2 us (13%)
  local copies, waits for them, and re-layouts  50.1 us (12%)
  blocking collectives  31.3 us (8%)
  between operations  14.7 us (4%)
  other arithmetic  7.43 us (2%)
    pallas_call x1, Pallas kernels, head_attention(): pl.pallas_call(kernel, grid=grid, in_specs=[pl.BlockSpec((bq, 1), lambda...  63.2 us
    reduce_scatter x1, waiting for transfers between devices, weight_gradient(): lax.psum_scatter(partial, 'ctx', scatter_dimension=0, axis_index_groups=a...  40.1 us
    ppermute x7, waiting for transfers between devices, send_hidden(): received.append(lax.ppermute(outgoing, 'dp', pairs))  34.9 us
    all_to_all x1, blocking collectives, local_body(): lax.all_to_all(grad_head.T.astype(jnp.bfloat16), 'ctx', split_axis=0, con...  31.3 us
    reduce_scatter x1, waiting for transfers between devices, weight_gradient(): lax.psum_scatter(reduced, 'ctx', scatter_dimension=0, axis_index_groups=a...  29.6 us
    ppermute x7, starting transfers between devices, send_hidden(): received.append(lax.ppermute(outgoing, 'dp', pairs))  25.4 us
    all_to_all x1, waiting for transfers between devices, local_body(): lax.all_to_all(copies, 'ctx', split_axis=1, concat_axis=0, tiled=True)  23.7 us
    all_to_all x1, waiting for transfers between devices, local_body(): lax.all_to_all(query_matrix_rows, 'ctx', split_axis=1, concat_axis=0, til...  22.7 us
  transfers between devices with their start and end apart: 16, of which 12 were waited for; matrix products, arithmetic and copies ran while one was open for 11% of the time, Pallas kernels for 0%

profile of v1, /device:TPU:0, one launch (start us, length us, event | category | flops | bytes accessed | tf_op | source)
XLA Modules:
  0.0 411.9 jit_solution(3738533118411880322)
XLA Ops:
  7.2 1.7 copy.101
  8.9 1.5 copy.75
  10.4 7.3 %all-to-all-start = ((bf16[128,16,384]{2,0,1:T(8,128)(2,1)}), bf16[128,16,384]{2,0,1:T(8,128)(2,1)S(1)}, u32[]{:S(2)}, u32[]{:S(2)}) async-start(bf16[128,16,384]{2,0,1:T(8,128)(2,1)} %copy.75), calls=%async_computation | async-start | bytes 3145728 | tf_op jit(solution)/shard_map/all_to_all | solution.py:198
  18.0 1.5 copy.76
  19.5 22.7 %all-to-all-done = bf16[128,16,384]{2,0,1:T(8,128)(2,1)S(1)} async-done(((bf16[128,16,384]{2,0,1:T(8,128)(2,1)}), bf16[128,16,384]{2,0,1:T(8,128)(2,1)S(1)}, u32[]{:S(2)}, u32[]{:S(2)}) %all-to-all-start) | async-done | bytes 1572896 | tf_op jit(solution)/shard_map/all_to_all | solution.py:198
  42.2 4.4 %all-to-all-start.1 = ((bf16[128,16,384]{2,0,1:T(8,128)(2,1)}), bf16[128,16,384]{2,0,1:T(8,128)(2,1)}, u32[]{:S(2)}, u32[]{:S(2)}) async-start(bf16[128,16,384]{2,0,1:T(8,128)(2,1)} %copy.76), calls=%async_computation.1 | async-start | bytes 3145728 | tf_op jit(solution)/shard_map/all_to_all | solution.py:199
  47.1 21.7 %all-to-all-done.1 = bf16[128,16,384]{2,0,1:T(8,128)(2,1)} async-done(((bf16[128,16,384]{2,0,1:T(8,128)(2,1)}), bf16[128,16,384]{2,0,1:T(8,128)(2,1)}, u32[]{:S(2)}, u32[]{:S(2)}) %all-to-all-start.1) | async-done | bytes 1572896 | tf_op jit(solution)/shard_map/all_to_all | solution.py:199
  68.8 1.5 broadcast_in_dim.24
  70.3 3.8 all-to-all-start.2
  76.2 1.4 copy.78.qdoc_ref
  77.6 1.3 convert_reduce_fusion
  79.5 23.7 %all-to-all-done.2 = bf16[256,16,256]{2,0,1:T(8,128)(2,1)S(1)} async-done(((bf16[256,16,256]{2,0,1:T(8,128)(2,1)}), bf16[256,16,256]{2,0,1:T(8,128)(2,1)S(1)}, u32[]{:S(2)}, u32[]{:S(2)}) %all-to-all-start.2) | async-done | bytes 2097184 | tf_op jit(solution)/shard_map/all_to_all | solution.py:200
  103.3 1.3 copy-done
  104.6 63.2 %band_attention.1 = (bf16[2048,384]{1,0:T(8,128)(2,1)}, bf16[2048,384]{1,0:T(8,128)(2,1)}, f32[256,4096]{1,0:T(8,128)}) custom-call(s32[2048,1]{1,0:T(8,128)} %copy.78.qdoc_ref, s32[1,4096]{1,0:T(1,128)} %compare_select_fusion.kdoc_ref, bf16[2048,384]{1,0:T(8,128)(2,1)} %bitcast.76, bf16[2048,384]{1,0:T(8,128)(2,1)} %bitcast.8.go_ref, bf16[4096,256]{1,0:T(8,128)(2,1)} %bitcast.71), custom_call_target="tpu_custom_call" | custom-call | flops 24159191040 | bytes 12582912 | tf_op jit(solution)/shard_map/band_attention/pallas_call | solution.py:76
  167.8 2.5 convert_element_type.37
  170.5 31.3 %all_to_all.130 = bf16[16,256,256]{1,2,0:T(8,128)(2,1)S(1)} all-to-all(bf16[16,256,256]{1,2,0:T(8,128)(2,1)S(1)} %bitcast.66), channel_id=1, replica_groups=mesh['dp'=8,'ctx'=16] {'ctx'}, dimensions={0} | all-to-all | bytes 4194304 | tf_op jit(solution)/shard_map/all_to_all | solution.py:211
  202.1 1.0 copy.83
  203.2 8.7 %copy.84 = bf16[1,256,12288]{1,2,0:T(8,128)(2,1)} copy(bf16[1,256,12288]{2,1,0:T(8,128)(2,1)} %param.8) | data formatting | bytes 12582912 | tf_op args[2]
  211.9 6.3 %copy.85 = bf16[8,256,4,4,96]{1,4,3,2,0:T(8,128)(2,1)} copy(bf16[8,256,4,4,96]{1,4,0,2,3:T(8,128)(2,1)} %bitcast.64) | data formatting | bytes 12582912 | tf_op jit(solution)/shard_map/transpose | solution.py:158
  218.3 4.7 %constant_dynamic-slice_fusion = (bf16[1,256,1536]{1,2,0:T(8,128)(2,1)S(1)}, bf16[1,256,1536]{1,2,0:T(8,128)(2,1)}, bf16[1,256,1536]{1,2,0:T(8,128)(2,1)}, bf16[...) fusion(bf16[8,256,1536]{1,2,0:T(8,128)(2,1)} %bitcast.63, ...), kind=kLoop, calls=%fused_computation.9 | loop fusion | bytes 12582944 | tf_op jit(solution)/shard_map/jit(dynamic_index_in_dim)/dynamic_slice | solution.py:163
  223.0 1.2 copy.87
  224.2 1.2 copy.88
  225.4 1.8 collective-permute-start.1
  227.1 4.4 %all-to-all-start.3 = ((bf16[16,128,384]{2,1,0:T(8,128)(2,1)}), bf16[16,128,384]{2,1,0:T(8,128)(2,1)}, u32[]{:S(2)}, u32[]{:S(2)}) async-start(bf16[16,128,384]{2,1,0:T(8,128)(2,1)} %bitcast.74), calls=%async_computation.3 | async-start | bytes 3145728 | tf_op jit(solution)/shard_map/all_to_all | solution.py:210
  231.6 1.1 copy.89
  232.7 2.9 collective-permute-start.2
  235.6 2.3 copy.90
  237.9 1.3 collective-permute-start.3
  239.2 2.3 copy.91
  241.4 2.3 collective-permute-start.4
  243.8 2.4 copy.92
  246.1 1.2 copy.93
  247.3 1.3 collective-permute-done.refs_1_
  250.0 16.2 %collective-permute-start.6 = (bf16[256,1536]{1,0:T(8,128)(2,1)}, bf16[256,1536]{1,0:T(8,128)(2,1)}, u32[]{:S(2)}, u32[]{:S(2)}) collective-permute-start(bf16[256,1536]{1,0:T(8,128)(2,1)} %bitcast.81), channel_id=1, source_target_pairs={{0,112},{16,0},{32,16},{48,32},{64,48},{80,64},{96,80},{112,96},{1... | collective-permute-start | bytes 2359304 | tf_op jit(solution)/shard_map/ppermute | solution.py:165
  266.2 1.4 copy.86
  267.6 2.8 copy.100
  270.4 12.2 %collective-permute-done.2.refs_3_ = bf16[256,1536]{1,0:T(8,128)(2,1)S(1)} collective-permute-done((bf16[256,1536]{1,0:T(8,128)(2,1)}, bf16[256,1536]{1,0:T(8,128)(2,1)S(1)}, u32[]{:S(2)}, u32[]{:S(2)}) %collective-permute-start.2) | collective-permute-done | bytes 786464 | tf_op jit(solution)/shard_map/ppermute | solution.py:165
  282.7 1.2 collective-permute-done.3.refs_4_
  283.8 12.9 %collective-permute-done.4.refs_5_ = bf16[256,1536]{1,0:T(8,128)(2,1)} collective-permute-done((bf16[256,1536]{1,0:T(8,128)(2,1)}, bf16[256,1536]{1,0:T(8,128)(2,1)}, u32[]{:S(2)}, u32[]{:S(2)}) %collective-permute-start.4) | collective-permute-done | bytes 786464 | tf_op jit(solution)/shard_map/ppermute | solution.py:165
  296.7 6.8 %collective-permute-done.6.refs_7_ = bf16[256,1536]{1,0:T(8,128)(2,1)} collective-permute-done((bf16[256,1536]{1,0:T(8,128)(2,1)}, bf16[256,1536]{1,0:T(8,128)(2,1)}, u32[]{:S(2)}, u32[]{:S(2)}) %collective-permute-start.6) | collective-permute-done | bytes 786464 | tf_op jit(solution)/shard_map/ppermute | solution.py:165
  303.6 10.8 %weight_product.1 = bf16[1536,1024]{1,0:T(8,128)(2,1)} custom-call(s32[1]{0:T(128)} %bitcast.19.me_ref, bf16[256,1536]{1,0:T(8,128)(2,1)S(1)} %bitcast.62, bf16[256,1536]{1,0:T(8,128)(2,1)S(1)} %collective-permute-done.refs_1_, bf16[256,1536]{1,0:T(8,128)(2,1)S(1)} %collective-permute-done.1.refs_2_, bf16[256,1536]{1,0:T(8,128)(2,1)S(1)} %collective-permute-done.2.refs_3_, ...), custom_call_target="tpu_custom_call" | custom-call | flops 6442450944 | bytes 13631488 | tf_op jit(solution)/shard_map/weight_product/pallas_call | solution.py:132
  314.5 40.1 %reduce-scatter.3.cloned.1.call-done = bf16[384,1024]{1,0:T(8,128)(2,1)} async-done(((bf16[1536,1024]{1,0:T(8,128)(2,1)}), bf16[384,1024]{1,0:T(8,128)(2,1)}) %reduce-scatter.3.cloned.1.call-update) | async-done | bytes 786448 | tf_op jit(solution)/shard_map/reduce_scatter | solution.py:175
  354.6 5.3 %all-to-all-start.5 = ((bf16[16,128,384]{2,1,0:T(8,128)(2,1)}), bf16[16,128,384]{2,1,0:T(8,128)(2,1)S(1)}, u32[]{:S(2)}, u32[]{:S(2)}) async-start(bf16[16,128,384]{2,1,0:T(8,128)(2,1)} %bitcast.31), calls=%async_computation.6 | async-start | bytes 3145728 | tf_op jit(solution)/shard_map/all_to_all | solution.py:177
  359.9 29.6 %reduce-scatter.5.cloned.1.call-done = bf16[96,1024]{1,0:T(8,128)(2,1)} async-done(((bf16[384,1024]{1,0:T(8,128)(2,1)}), bf16[96,1024]{1,0:T(8,128)(2,1)}) %reduce-scatter.5.cloned.1.call-update) | async-done | bytes 196624 | tf_op jit(solution)/shard_map/reduce_scatter | solution.py:178
  389.5 1.7 copy_bitcast_fusion.1
  391.2 4.5 %all-to-all-start.6 = ((f32[96,8,128]{2,0,1:T(8,128)}), f32[96,8,128]{2,0,1:T(8,128)S(1)}, u32[]{:S(2)}, u32[]{:S(2)}) async-start(f32[96,8,128]{2,0,1:T(8,128)} %copy_bitcast_fusion.1), calls=%async_computation.8 | async-start | bytes 786432 | tf_op jit(solution)/shard_map/all_to_all | solution.py:179
  396.6 1.6 broadcast_in_dim.26
  398.2 6.4 %all-to-all-done.6 = f32[96,8,128]{2,0,1:T(8,128)S(1)} async-done(((f32[96,8,128]{2,0,1:T(8,128)}), f32[96,8,128]{2,0,1:T(8,128)S(1)}, u32[]{:S(2)}, u32[]{:S(2)}) %all-to-all-start.6) | async-done | bytes 393248 | tf_op jit(solution)/shard_map/all_to_all | solution.py:179
  (38 shorter events, 6.5 us)
Async XLA Ops:
  10.4 7.3 %copy-start.1 = (bf16[1,128,6144]{2,1,0:T(8,128)(2,1)S(1)}, bf16[1,128,6144]{2,1,0:T(8,128)(2,1)}, u32[]{:S(2)}) copy-start(bf16[1,128,6144]{2,1,0:T(8,128)(2,1)} %param.9) | copy-start | bytes 4718596
  10.4 31.8 %all-to-all-start = ((bf16[128,16,384]{2,0,1:T(8,128)(2,1)}), bf16[128,16,384]{2,0,1:T(8,128)(2,1)S(1)}, u32[]{:S(2)}, u32[]{:S(2)}) async-start(bf16[128,16,384]{2,0,1:T(8,128)(2,1)} %copy.75), calls=%async_computation | async-start | bytes 3145728 | tf_op jit(solution)/shard_map/all_to_all | solution.py:198
  19.5 27.1 %copy-start.3 = (bf16[1,256,1024]{2,1,0:T(8,128)(2,1)S(1)}, bf16[1,256,1024]{2,1,0:T(8,128)(2,1)}, u32[]{:S(2)}) copy-start(bf16[1,256,1024]{2,1,0:T(8,128)(2,1)} %param.7) | copy-start | bytes 1572868
  42.2 4.8 %copy-start.2 = (bf16[128,16,384]{2,0,1:T(8,128)(2,1)}, bf16[128,16,384]{2,0,1:T(8,128)(2,1)S(1)}, u32[]{:S(2)}) copy-start(bf16[128,16,384]{2,0,1:T(8,128)(2,1)S(1)} %all-to-all-done) | copy-start | bytes 4718596
  42.2 26.6 %all-to-all-start.1 = ((bf16[128,16,384]{2,0,1:T(8,128)(2,1)}), bf16[128,16,384]{2,0,1:T(8,128)(2,1)}, u32[]{:S(2)}, u32[]{:S(2)}) async-start(bf16[128,16,384]{2,0,1:T(8,128)(2,1)} %copy.76), calls=%async_computation.1 | async-start | bytes 3145728 | tf_op jit(solution)/shard_map/all_to_all | solution.py:199
  70.3 3.9 copy-start.4
  70.3 32.9 %all-to-all-start.2 = ((bf16[256,16,256]{2,0,1:T(8,128)(2,1)}), bf16[256,16,256]{2,0,1:T(8,128)(2,1)S(1)}, u32[]{:S(2)}, u32[]{:S(2)}) async-start(bf16[256,16,256]{2,0,1:T(8,128)(2,1)} %bitcast.9), calls=%async_computation.2 | async-start | bytes 4194304 | tf_op jit(solution)/shard_map/all_to_all | solution.py:200
  74.2 196.2 %all-gather.2.cloned.1.call-start = ((), (), s32[]{:S(2)}) async-start(), calls=%async_computation.9 | async-start | bytes 4718592 | tf_op jit(solution)/shard_map/all_gather | solution.py:221
  103.3 1.3 copy-start
  224.2 24.4 %collective-permute-start = (bf16[256,1536]{1,0:T(8,128)(2,1)}, bf16[256,1536]{1,0:T(8,128)(2,1)S(1)}, u32[]{:S(2)}, u32[]{:S(2)}) collective-permute-start(bf16[256,1536]{1,0:T(8,128)(2,1)} %bitcast.84), channel_id=1, source_target_pairs={{0,16},{16,32},{32,48},{48,64},{64,80},{80,96},{96,112},{112,0},{1... | collective-permute-start | bytes 2359304 | tf_op jit(solution)/shard_map/ppermute | solution.py:165
  225.4 24.7 %collective-permute-start.1 = (bf16[256,1536]{1,0:T(8,128)(2,1)}, bf16[256,1536]{1,0:T(8,128)(2,1)S(1)}, u32[]{:S(2)}, u32[]{:S(2)}) collective-permute-start(bf16[256,1536]{1,0:T(8,128)(2,1)} %bitcast.83), channel_id=1, source_target_pairs={{0,32},{16,48},{32,64},{48,80},{64,96},{80,112},{96,0},{112,16},{1... | collective-permute-start | bytes 2359304 | tf_op jit(solution)/shard_map/ppermute | solution.py:165
  227.1 40.5 %all-to-all-start.3 = ((bf16[16,128,384]{2,1,0:T(8,128)(2,1)}), bf16[16,128,384]{2,1,0:T(8,128)(2,1)}, u32[]{:S(2)}, u32[]{:S(2)}) async-start(bf16[16,128,384]{2,1,0:T(8,128)(2,1)} %bitcast.74), calls=%async_computation.3 | async-start | bytes 3145728 | tf_op jit(solution)/shard_map/all_to_all | solution.py:210
  231.5 123.0 %reduce-scatter.3.cloned.1.call-start = ((), (), s32[]{:S(2)}) async-start(), calls=%async_computation.10 | async-start | bytes 3932160 | tf_op jit(solution)/shard_map/reduce_scatter | solution.py:175
  232.7 49.9 %collective-permute-start.2 = (bf16[256,1536]{1,0:T(8,128)(2,1)}, bf16[256,1536]{1,0:T(8,128)(2,1)S(1)}, u32[]{:S(2)}, u32[]{:S(2)}) collective-permute-start(bf16[256,1536]{1,0:T(8,128)(2,1)} %bitcast.78), channel_id=1, source_target_pairs={{0,48},{16,64},{32,80},{48,96},{64,112},{80,0},{96,16},{112,32},{1... | collective-permute-start | bytes 2359304 | tf_op jit(solution)/shard_map/ppermute | solution.py:165
  237.9 45.9 %collective-permute-start.3 = (bf16[256,1536]{1,0:T(8,128)(2,1)}, bf16[256,1536]{1,0:T(8,128)(2,1)}, u32[]{:S(2)}, u32[]{:S(2)}) collective-permute-start(bf16[256,1536]{1,0:T(8,128)(2,1)} %bitcast.79), channel_id=1, source_target_pairs={{0,64},{16,80},{32,96},{48,112},{64,0},{80,16},{96,32},{112,48},{1... | collective-permute-start | bytes 2359304 | tf_op jit(solution)/shard_map/ppermute | solution.py:165
  241.4 55.3 %collective-permute-start.4 = (bf16[256,1536]{1,0:T(8,128)(2,1)}, bf16[256,1536]{1,0:T(8,128)(2,1)}, u32[]{:S(2)}, u32[]{:S(2)}) collective-permute-start(bf16[256,1536]{1,0:T(8,128)(2,1)} %bitcast.80), channel_id=1, source_target_pairs={{0,80},{16,96},{32,112},{48,0},{64,16},{80,32},{96,48},{112,64},{1... | collective-permute-start | bytes 2359304 | tf_op jit(solution)/shard_map/ppermute | solution.py:165
  248.6 48.2 %collective-permute-start.5 = (bf16[256,1536]{1,0:T(8,128)(2,1)}, bf16[256,1536]{1,0:T(8,128)(2,1)}, u32[]{:S(2)}, u32[]{:S(2)}) collective-permute-start(bf16[256,1536]{1,0:T(8,128)(2,1)} %bitcast.82), channel_id=1, source_target_pairs={{0,96},{16,112},{32,0},{48,16},{64,32},{80,48},{96,64},{112,80},{1... | collective-permute-start | bytes 2359304 | tf_op jit(solution)/shard_map/ppermute | solution.py:165
  250.0 53.6 %collective-permute-start.6 = (bf16[256,1536]{1,0:T(8,128)(2,1)}, bf16[256,1536]{1,0:T(8,128)(2,1)}, u32[]{:S(2)}, u32[]{:S(2)}) collective-permute-start(bf16[256,1536]{1,0:T(8,128)(2,1)} %bitcast.81), channel_id=1, source_target_pairs={{0,112},{16,0},{32,16},{48,32},{64,48},{80,64},{96,80},{112,96},{1... | collective-permute-start | bytes 2359304 | tf_op jit(solution)/shard_map/ppermute | solution.py:165
  314.4 75.1 %reduce-scatter.5.cloned.1.call-start = ((), (), s32[]{:S(2)}) async-start(), calls=%async_computation.11 | async-start | bytes 983040 | tf_op jit(solution)/shard_map/reduce_scatter | solution.py:178
  354.6 36.6 %all-to-all-start.5 = ((bf16[16,128,384]{2,1,0:T(8,128)(2,1)}), bf16[16,128,384]{2,1,0:T(8,128)(2,1)S(1)}, u32[]{:S(2)}, u32[]{:S(2)}) async-start(bf16[16,128,384]{2,1,0:T(8,128)(2,1)} %bitcast.31), calls=%async_computation.6 | async-start | bytes 3145728 | tf_op jit(solution)/shard_map/all_to_all | solution.py:177
  391.2 13.4 %all-to-all-start.6 = ((f32[96,8,128]{2,0,1:T(8,128)}), f32[96,8,128]{2,0,1:T(8,128)S(1)}, u32[]{:S(2)}, u32[]{:S(2)}) async-start(f32[96,8,128]{2,0,1:T(8,128)} %copy_bitcast_fusion.1), calls=%async_computation.8 | async-start | bytes 786432 | tf_op jit(solution)/shard_map/all_to_all | solution.py:179
Sparse Core Ops, SparseCore 0:
  203.3 34.0 all-gather.1
  314.5 39.9 reduce-scatter.2
  357.0 32.4 reduce-scatter.4
